TPU v7x, 256 devices: a whole 4x4x8 slice. The times are simulated.
256 devices in a mesh: seq: 32 (over z, x), head: 8 (over y, core).
Axes of the slice: x: 4, y: 4, z: 8, core: 2. Of those that a mesh axis runs over, the one named last changes fastest.
Arguments:
- queries: bfloat16 [16384, 4096], P('seq', 'head'), may hold values from -6 to 6
- key_rows: bfloat16 [16384, 4096], P('seq', 'head'), may hold values from -6 to 6
- value_rows: bfloat16 [16384, 4096], P('seq', 'head'), may hold values from -18 to 18
- out_grad: bfloat16 [16384, 4096], P('seq', 'head'), may hold values from -6 to 6
- log_decay: float32 [32, 16384], P('head', 'seq'), may hold values from -0.6 to 0
Outputs:
- query_gradient: bfloat16 [16384, 4096], P('seq', 'head')
- key_grad: bfloat16 [16384, 4096], P('seq', 'head')
- value_grad: bfloat16 [16384, 4096], P('seq', 'head')
All inputs are finite; a program needn't handle non-finite values.
Results may differ from a plain program's by a relative error of at most 0.006.
Values sent between devices are 32-bit elements; how exact they have to be, the bound alone decides.
No kernel may reach another device: no remote copies, remote signals or barrier semaphores. Data moves between devices by JAX's collectives and lax.ppermute only.
A program may use at most 64 MiB of HBM per device.

v0:
```python
import jax
import jax.numpy as jnp
from jax import lax
from jax.sharding import PartitionSpec as P

HEAD_COUNT = 32
DH = 128
BLOCK = 128
epsilon = 1e-06
highest = lax.Precision.HIGHEST


def shards(queries, key_rows, value_rows, out_grad, log_decay):
    tok_rows, row_width = queries.shape
    heads_dev = log_decay.shape[0]
    head_size = row_width // heads_dev
    blocks = tok_rows // BLOCK
    total_width = HEAD_COUNT * DH
    block_shape = (blocks, BLOCK, heads_dev, head_size)
    query_block_rows = queries.reshape(block_shape)
    key_blocks = key_rows.reshape(block_shape)
    value_block_rows = value_rows.reshape(block_shape)
    grad_blocks = out_grad.reshape(block_shape)
    decay_blocks = jnp.transpose(log_decay.reshape(heads_dev, blocks, BLOCK), (1, 2, 0))
    inside_block_mask = jnp.cumsum(decay_blocks, axis=1)
    totals = inside_block_mask[:, -1, :]
    before = jnp.cumsum(totals, axis=0) - totals
    shard_total = jnp.sum(totals, axis=0)
    token_positions = jnp.arange(BLOCK)
    causal = (token_positions[:, None] >= token_positions[None, :]).astype(jnp.float32)
    within_heads = jnp.transpose(inside_block_mask, (0, 2, 1))
    exponent = within_heads[:, :, :, None] - within_heads[:, :, None, :]
    decay_mask = jnp.exp(jnp.minimum(exponent, 0.0)) * causal
    scores = jnp.einsum(
        "nihd,njhd->nhij", query_block_rows, key_blocks, preferred_element_type=jnp.float32
    )
    attention_weights = (scores * decay_mask).astype(jnp.bfloat16)
    intra_out = jnp.einsum(
        "nhij,njhd->nihd", attention_weights, value_block_rows, preferred_element_type=jnp.float32
    )
    to_end = jnp.exp(totals[:, None, :] - inside_block_mask)
    keys_scaled = (to_end[..., None] * key_blocks).astype(jnp.bfloat16)
    block_terms = jnp.einsum(
        "njhd,njhe->nhde", keys_scaled, value_block_rows, preferred_element_type=jnp.float32
    )
    block_ids = jnp.arange(blocks)
    earlier_blocks = (block_ids[:, None] > block_ids[None, :]).astype(jnp.float32)
    forward_exp = before[:, None, :] - before[None, :, :] - totals[None, :, :]
    forward_mix = jnp.exp(jnp.minimum(forward_exp, 0.0)) * earlier_blocks[:, :, None]
    local_states = jnp.einsum("nmh,mhde->nhde", forward_mix, block_terms, precision=highest)
    shard_state = jnp.einsum(
        "mh,mhde->hde",
        jnp.exp(shard_total[None, :] - before - totals),
        block_terms,
        precision=highest,
    )
    all_totals, all_states = (
        lax.all_gather(shard_total[None], "seq", axis=0, tiled=True),
        lax.all_gather(shard_state[None], "seq", axis=0, tiled=True),
    )
    seq_ranks = lax.axis_size("seq")
    my_rank = lax.axis_index("seq")
    starts = jnp.cumsum(all_totals, axis=0) - all_totals
    my_start = lax.dynamic_index_in_dim(starts, my_rank, 0, keepdims=False)
    rank_ids = jnp.arange(seq_ranks)
    reach_log = my_start[None, :] - starts - all_totals
    mixing = jnp.exp(jnp.minimum(reach_log, 0.0)) * (rank_ids < my_rank)[:, None].astype(
        jnp.float32
    )
    incoming = jnp.einsum("rh,rhde->hde", mixing, all_states, precision=highest)
    states = local_states + jnp.exp(before)[:, :, None, None] * incoming[None]
    backward_state = states.astype(jnp.bfloat16)
    inter_out = jnp.einsum(
        "nihd,nhde->nihe", query_block_rows, backward_state, preferred_element_type=jnp.float32
    )
    attention_output = intra_out + jnp.exp(inside_block_mask)[..., None] * inter_out
    square = jnp.sum(attention_output * attention_output, axis=(2, 3))
    square_total = lax.psum(square, "head")
    inv_rms = lax.rsqrt(square_total / total_width + epsilon)
    normed = attention_output * inv_rms[:, :, None, None]
    cross_local = jnp.sum(grad_blocks.astype(jnp.float32) * normed, axis=(2, 3))
    cross_total = lax.psum(cross_local, "head")
    mean_cross = cross_total / total_width
    attention_gradient = (
        inv_rms[:, :, None, None]
        * (grad_blocks.astype(jnp.float32) - normed * mean_cross[:, :, None, None])
    ).astype(jnp.bfloat16)
    score_gradient = jnp.einsum(
        "nihe,njhe->nhij", attention_gradient, value_block_rows, preferred_element_type=jnp.float32
    )
    grad_probs = (score_gradient * decay_mask).astype(jnp.bfloat16)
    query_gradient = jnp.einsum(
        "nhij,njhd->nihd", grad_probs, key_blocks, preferred_element_type=jnp.float32
    )
    query_gradient = query_gradient + jnp.exp(inside_block_mask)[..., None] * jnp.einsum(
        "nihe,nhde->nihd", attention_gradient, backward_state, preferred_element_type=jnp.float32
    )
    key_intra = jnp.einsum(
        "nhij,nihd->njhd", grad_probs, query_block_rows, preferred_element_type=jnp.float32
    )
    value_within_block = jnp.einsum(
        "nhij,nihe->njhe", attention_weights, attention_gradient, preferred_element_type=jnp.float32
    )
    scaled_query_rows = (jnp.exp(inside_block_mask)[..., None] * query_block_rows).astype(
        jnp.bfloat16
    )
    backward_terms = jnp.einsum(
        "nihd,nihe->nhde", scaled_query_rows, attention_gradient, preferred_element_type=jnp.float32
    )
    later_blocks = (block_ids[:, None] < block_ids[None, :]).astype(jnp.float32)
    backward_exp = before[None, :, :] - before[:, None, :] - totals[:, None, :]
    backward_mix = jnp.exp(jnp.minimum(backward_exp, 0.0)) * later_blocks[:, :, None]
    local_back = jnp.einsum("nmh,mhde->nhde", backward_mix, backward_terms, precision=highest)
    shard_back = jnp.einsum("mh,mhde->hde", jnp.exp(before), backward_terms, precision=highest)
    shard_piece = lax.all_gather(shard_back[None], "seq", axis=0, tiled=True)
    piece_rows = shard_piece.shape[0]
    piece_ranks = jnp.arange(piece_rows)
    reach_log = starts - my_start[None, :] - shard_total[None, :]
    mixing = jnp.exp(jnp.minimum(reach_log, 0.0)) * (piece_ranks > my_rank)[:, None].astype(
        jnp.float32
    )
    later_state = jnp.einsum("rh,rhde->hde", mixing, shard_piece, precision=highest)
    back_states = (
        local_back
        + jnp.exp(shard_total[None, :] - before - totals)[:, :, None, None] * later_state[None]
    )
    back_b = back_states.astype(jnp.bfloat16)
    key_grad = key_intra + to_end[..., None] * jnp.einsum(
        "njhe,nhde->njhd", value_block_rows, back_b, preferred_element_type=jnp.float32
    )
    value_grad = value_within_block + to_end[..., None] * jnp.einsum(
        "njhd,nhde->njhe", key_blocks, back_b, preferred_element_type=jnp.float32
    )
    return (
        query_gradient.reshape(tok_rows, row_width).astype(jnp.bfloat16),
        key_grad.reshape(tok_rows, row_width).astype(jnp.bfloat16),
        value_grad.reshape(tok_rows, row_width).astype(jnp.bfloat16),
    )


def solution(mesh):
    return jax.shard_map(
        shards,
        mesh=mesh,
        in_specs=(
            P("seq", "head"),
            P("seq", "head"),
            P("seq", "head"),
            P("seq", "head"),
            P("head", "seq"),
        ),
        out_specs=(P("seq", "head"), P("seq", "head"), P("seq", "head")),
        check_vma=False,
    )
```

profile of v0, /device:TPU:1, one launch (start us, length us, event | category | flops | bytes accessed | tf_op | source)
XLA Modules:
  0.0 287.0 jit_solution(773826581241886380)
XLA Ops:
  13.2 3.1 %fusion.24 = f32[4,1,128,128]{3,1,2,0:T(1,128)} fusion(f32[4,4,1,1]{0,2,3,1:T(1,128)S(1)} %copy.132, f32[4,4,128,128]{3,2,1,0:T(8,128)S(1)} %fusion.27), kind=kOutput, calls=%fused_computation.42 | convolution fusion | flops 3145728 | bytes 1310784 | tf_op jit(solution)/shard_map/mh,mhde->hde/dot_general | solution.py:51
  18.7 64.9 %all-reduce = f32[128]{0:T(128)S(1)} all-reduce(f32[128]{0:T(128)S(1)} %dynamic-update-slice), channel_id=2, replica_groups=mesh['seq'=32,'head'=8] {'seq'}, use_global_device_ids=true, to_apply=%add | all-reduce | flops 128 | bytes 1024
  84.8 1.3 reshape.133
  86.1 1.6 copy.106
  89.2 1.5 convolution_bitcast_fusion.9
  90.7 26.8 %all-gather.6.cloned.1.call-done = f32[128,128,128]{2,1,0:T(8,128)} async-done(((f32[4,128,128]{2,1,0:T(8,128)}), f32[128,128,128]{2,1,0:T(8,128)}) %all-gather.6.cloned.1.call-update) | async-done | bytes 8388624 | tf_op jit(solution)/shard_map/all_gather | solution.py:59
  117.5 12.2 %fusion.2 = f32[4,1,128,128]{3,1,2,0:T(1,128)S(1)} fusion(f32[32,4,1,1]{0,2,3,1:T(1,128)S(1)} %copy.134, f32[32,4,128,128]{3,2,1,0:T(8,128)} %bitcast.121), kind=kOutput, calls=%fused_computation.2 | convolution fusion | flops 25165824 | bytes 8651264 | tf_op jit(solution)/shard_map/rh,rhde->hde/dot_general | solution.py:70
  129.7 2.7 fusion.18
  132.4 1.6 multiply_reduce_fusion.1
  134.1 13.2 %psum.14 = f32[4,128]{1,0:T(4,128)S(1)} all-reduce(f32[4,128]{1,0:T(4,128)S(1)} %get-tuple-element.13), channel_id=1, replica_groups=mesh['seq'=32,'head'=8] {'head'}, use_global_device_ids=true, to_apply=%region_5.6 | all-reduce | flops 512 | bytes 4096 | tf_op jit(solution)/shard_map/psum | solution.py:78
  147.4 14.1 %psum.15 = f32[4,128]{1,0:T(4,128)S(1)} all-reduce(f32[4,128]{1,0:T(4,128)S(1)} %multiply_reduce_fusion), channel_id=1, replica_groups=mesh['seq'=32,'head'=8] {'head'}, use_global_device_ids=true, to_apply=%region_7.8 | all-reduce | flops 512 | bytes 4096 | tf_op jit(solution)/shard_map/psum | solution.py:82
  162.5 1.6 fusion.28
  164.1 3.1 %fusion.21 = f32[4,1,128,128]{3,1,2,0:T(1,128)} fusion(f32[4,4,1,1]{0,2,3,1:T(1,128)S(1)} %copy.143, f32[4,4,128,128]{3,2,1,0:T(8,128)S(1)} %fusion.28), kind=kOutput, calls=%fused_computation.39 | convolution fusion | flops 3145728 | bytes 1310784 | tf_op jit(solution)/shard_map/mh,mhde->hde/dot_general | solution.py:114
  167.4 1.6 fusion.19
  170.4 2.3 fusion.14
  172.7 2.2 copy.113
  174.9 2.0 copy.196
  176.9 2.6 convolution_bitcast_fusion.2
  179.5 2.5 convolution_bitcast_fusion.4
  182.0 77.0 %all-gather.8.cloned.1.call-done = f32[128,128,128]{2,1,0:T(8,128)} async-done(((f32[4,128,128]{2,1,0:T(8,128)}), f32[128,128,128]{2,1,0:T(8,128)}) %all-gather.8.cloned.1.call-update) | async-done | bytes 8388624 | tf_op jit(solution)/shard_map/all_gather | solution.py:115
  259.0 12.3 %fusion = f32[4,1,128,128]{3,1,2,0:T(1,128)S(1)} fusion(f32[32,4,1,1]{0,2,3,1:T(1,128)S(1)} %copy.145, f32[32,4,128,128]{3,2,1,0:T(8,128)} %bitcast.122), kind=kOutput, calls=%fused_computation | convolution fusion | flops 25165824 | bytes 8651264 | tf_op jit(solution)/shard_map/rh,rhde->hde/dot_general | solution.py:122
  271.3 2.6 fusion.20
  274.3 1.7 fusion.15
  277.3 1.6 fusion.16
  (76 shorter events, 16.0 us)
Async XLA Ops:
  7.2 77.1 %copy-start.11 = (bf16[512,512]{1,0:T(8,128)(2,1)S(1)}, bf16[512,512]{1,0:T(8,128)(2,1)}, u32[]{:S(2)}) copy-start(bf16[512,512]{1,0:T(8,128)(2,1)} %param.5) | copy-start | bytes 1572868
  7.2 77.6 %copy-start.10 = (bf16[512,512]{1,0:T(8,128)(2,1)S(1)}, bf16[512,512]{1,0:T(8,128)(2,1)}, u32[]{:S(2)}) copy-start(bf16[512,512]{1,0:T(8,128)(2,1)} %param.8) | copy-start | bytes 1572868
  7.2 110.3 %all-gather.6.cloned.1.call-start = ((), (), s32[]{:S(2)}) async-start(), calls=%async_computation | async-start | bytes 8650752 | tf_op jit(solution)/shard_map/all_gather | solution.py:59
  12.1 1.1 copy-start.4
  16.3 242.7 %all-gather.8.cloned.1.call-start = ((), (), s32[]{:S(2)}) async-start(), calls=%async_computation.1 | async-start | bytes 8650752 | tf_op jit(solution)/shard_map/all_gather | solution.py:115
  84.7 45.0 %copy-start.2 = (bf16[4,128,4,128]{1,3,2,0:T(8,128)(2,1)}, bf16[4,128,4,128]{1,3,2,0:T(8,128)(2,1)S(1)}, u32[]{:S(2)}) copy-start(bf16[4,128,4,128]{1,3,2,0:T(8,128)(2,1)S(1)} %copy.116) | copy-start | bytes 1572868
  88.4 0.8 copy-start.8
  117.5 12.2 %copy-start.5 = (f32[4,4,128,128]{3,2,1,0:T(8,128)S(1)}, f32[4,4,128,128]{3,2,1,0:T(8,128)}, u32[]{:S(2)}) copy-start(f32[4,4,128,128]{3,2,1,0:T(8,128)} %copy-done.4) | copy-start | bytes 3145732
  117.5 14.9 %copy-start.6 = (f32[4,128,4,128]{1,3,2,0:T(8,128)S(1)}, f32[4,128,4,128]{1,3,2,0:T(8,128)}, u32[]{:S(2)}) copy-start(f32[4,128,4,128]{1,3,2,0:T(8,128)} %convolution_bitcast_fusion.9) | copy-start | bytes 3145732
  132.4 1.7 copy-start.7
  161.7 0.8 copy-start
  162.5 17.0 %copy-start.3 = (bf16[4,128,4,128]{1,3,2,0:T(8,128)(2,1)S(1)}, bf16[4,128,4,128]{1,3,2,0:T(8,128)(2,1)}, u32[]{:S(2)}) copy-start(bf16[4,128,4,128]{1,3,2,0:T(8,128)(2,1)} %copy-done.2) | copy-start | bytes 1572868
  164.1 12.7 %copy-start.1 = (bf16[4,128,4,128]{1,3,2,0:T(8,128)(2,1)S(1)}, bf16[4,128,4,128]{1,3,2,0:T(8,128)(2,1)}, u32[]{:S(2)}) copy-start(bf16[4,128,4,128]{1,3,2,0:T(8,128)(2,1)} %copy-done) | copy-start | bytes 1572868
  169.0 0.8 copy-start.9
Sparse Core Ops, SparseCore 0:
  16.4 101.0 all-gather.5
  167.3 91.5 all-gather.7
where the time goes:
time: 288 us; the launch traced here: 287 us
  waiting for transfers between devices  104 us (36%)
  blocking collectives  92.1 us (32%)
  matrix products  55.1 us (19%)
  local copies, waits for them, and re-layouts  19.9 us (7%)
  between operations  15 us (5%)
    all_gather x1, waiting for transfers between devices, shards(): shard_piece = lax.all_gather(shard_back[None], 'seq', axis=0, tiled=True)  77 us
    unnamed x1, blocking collectives  64.9 us
    all_gather x1, waiting for transfers between devices, shards(): lax.all_gather(shard_state[None], 'seq', axis=0, tiled=True)  26.8 us
    psum x1, blocking collectives, shards(): cross_total = lax.psum(cross_local, 'head')  14.1 us
    psum x1, blocking collectives, shards(): square_total = lax.psum(square, 'head')  13.2 us
    dot_general x1, matrix products, shards(): jnp.einsum('rh,rhde->hde', mixing, shard_piece, precision=highest)  12.3 us
    dot_general x1, matrix products, shards(): incoming = jnp.einsum('rh,rhde->hde', mixing, all_states, precision=highest)  12.2 us
    unnamed x30, local copies, waits for them, and re-layouts  8.71 us
  transfers between devices with their start and end apart: 2, of which 2 were waited for; matrix products, arithmetic and copies ran while one was open for 8% of the time, Pallas kernels for 0%

commit v1 on v0

--- a/solution.py
+++ b/solution.py
@@ -79,7 +79,7 @@
     inv_rms = lax.rsqrt(square_total / total_width + epsilon)
     normed = attention_output * inv_rms[:, :, None, None]
     cross_local = jnp.sum(grad_blocks.astype(jnp.float32) * normed, axis=(2, 3))
-    cross_total = lax.psum(cross_local, "head")
+    cross_total = jnp.sum(lax.all_gather(cross_local, "head"), 0)
     mean_cross = cross_total / total_width
     attention_gradient = (
         inv_rms[:, :, None, None]

time: 288 us -> 288 us (level)
    psum x1 -> x0, blocking collectives: 14.1 us -> none  [shards(): cross_total = lax.psum(cross_local, 'head')]
    all_gather x0 -> x1, blocking collectives: none -> 13.4 us  [shards(): cross_total = jnp.sum(lax.all_gather(cross_local, 'head'), 0)]
where the time goes in v1:
time: 288 us
  waiting for transfers between devices  105 us (36%)
  blocking collectives  91.5 us (32%)
  matrix products  54.9 us (19%)
  local copies, waits for them, and re-layouts  19.9 us (7%)
  between operations  15 us (5%)
    all_gather x1, waiting for transfers between devices, shards(): shard_piece = lax.all_gather(shard_back[None], 'seq', axis=0, tiled=True)  78.4 us
    unnamed x1, blocking collectives  64.9 us
    all_gather x1, waiting for transfers between devices, shards(): lax.all_gather(shard_state[None], 'seq', axis=0, tiled=True)  26.8 us
    all_gather x1, blocking collectives, shards(): cross_total = jnp.sum(lax.all_gather(cross_local, 'head'), 0)  13.4 us
    psum x1, blocking collectives, shards(): square_total = lax.psum(square, 'head')  13.2 us
    dot_general x1, matrix products, shards(): incoming = jnp.einsum('rh,rhde->hde', mixing, all_states, precision=highest)  12.2 us
    dot_general x1, matrix products, shards(): jnp.einsum('rh,rhde->hde', mixing, shard_piece, precision=highest)  12 us
    unnamed x30, local copies, waits for them, and re-layouts  8.69 us
  transfers between devices with their start and end apart: 2, of which 2 were waited for; matrix products, arithmetic and copies ran while one was open for 8% of the time, Pallas kernels for 0%

profile of v1, /device:TPU:1, one launch (start us, length us, event | category | flops | bytes accessed | tf_op | source)
XLA Modules:
  0.0 287.6 jit_solution(13130188976721603181)
XLA Ops:
  13.2 3.1 %fusion.24 = f32[4,1,128,128]{3,1,2,0:T(1,128)} fusion(f32[4,4,1,1]{0,2,3,1:T(1,128)S(1)} %copy.132, f32[4,4,128,128]{3,2,1,0:T(8,128)S(1)} %fusion.27), kind=kOutput, calls=%fused_computation.42 | convolution fusion | flops 3145728 | bytes 1310784 | tf_op jit(solution)/shard_map/mh,mhde->hde/dot_general | solution.py:51
  18.7 64.9 %all-reduce = f32[128]{0:T(128)S(1)} all-reduce(f32[128]{0:T(128)S(1)} %dynamic-update-slice), channel_id=2, replica_groups=mesh['seq'=32,'head'=8] {'seq'}, use_global_device_ids=true, to_apply=%add | all-reduce | flops 128 | bytes 1024
  84.8 1.3 reshape.135
  86.1 1.6 copy.106
  89.2 1.5 convolution_bitcast_fusion.9
  90.7 26.8 %all-gather.8.cloned.1.call-done = f32[128,128,128]{2,1,0:T(8,128)} async-done(((f32[4,128,128]{2,1,0:T(8,128)}), f32[128,128,128]{2,1,0:T(8,128)}) %all-gather.8.cloned.1.call-update) | async-done | bytes 8388624 | tf_op jit(solution)/shard_map/all_gather | solution.py:59
  117.5 12.2 %fusion.2 = f32[4,1,128,128]{3,1,2,0:T(1,128)S(1)} fusion(f32[32,4,1,1]{0,2,3,1:T(1,128)S(1)} %copy.134, f32[32,4,128,128]{3,2,1,0:T(8,128)} %bitcast.122), kind=kOutput, calls=%fused_computation.2 | convolution fusion | flops 25165824 | bytes 8651264 | tf_op jit(solution)/shard_map/rh,rhde->hde/dot_general | solution.py:70
  129.7 2.7 fusion.18
  132.4 1.6 multiply_reduce_fusion.1
  134.1 13.2 %psum.7 = f32[4,128]{1,0:T(4,128)S(1)} all-reduce(f32[4,128]{1,0:T(4,128)S(1)} %get-tuple-element.13), channel_id=1, replica_groups=mesh['seq'=32,'head'=8] {'head'}, use_global_device_ids=true, to_apply=%region_5.6 | all-reduce | flops 512 | bytes 4096 | tf_op jit(solution)/shard_map/psum | solution.py:78
  147.4 13.4 %all-gather.4 = f32[8,4,128]{2,1,0:T(4,128)S(1)} all-gather(f32[1,4,128]{2,1,0:T(4,128)S(1)} %bitcast.144), channel_id=4, replica_groups=mesh['seq'=32,'head'=8] {'head'}, dimensions={0}, use_global_device_ids=true | all-gather | bytes 18432 | tf_op jit(solution)/shard_map/all_gather | solution.py:82
  161.9 1.6 fusion.28
  163.5 3.1 %fusion.21 = f32[4,1,128,128]{3,1,2,0:T(1,128)} fusion(f32[4,4,1,1]{0,2,3,1:T(1,128)S(1)} %copy.143, f32[4,4,128,128]{3,2,1,0:T(8,128)S(1)} %fusion.28), kind=kOutput, calls=%fused_computation.39 | convolution fusion | flops 3145728 | bytes 1310784 | tf_op jit(solution)/shard_map/mh,mhde->hde/dot_general | solution.py:114
  166.8 1.6 fusion.19
  169.7 2.3 fusion.14
  172.1 2.2 copy.113
  174.3 1.9 copy.196
  176.2 2.6 convolution_bitcast_fusion.2
  178.8 2.5 convolution_bitcast_fusion.4
  181.4 78.4 %all-gather.10.cloned.1.call-done = f32[128,128,128]{2,1,0:T(8,128)} async-done(((f32[4,128,128]{2,1,0:T(8,128)}), f32[128,128,128]{2,1,0:T(8,128)}) %all-gather.10.cloned.1.call-update) | async-done | bytes 8388624 | tf_op jit(solution)/shard_map/all_gather | solution.py:115
  259.7 12.0 %fusion = f32[4,1,128,128]{3,1,2,0:T(1,128)S(1)} fusion(f32[32,4,1,1]{0,2,3,1:T(1,128)S(1)} %copy.145, f32[32,4,128,128]{3,2,1,0:T(8,128)} %bitcast.123), kind=kOutput, calls=%fused_computation | convolution fusion | flops 25165824 | bytes 8651264 | tf_op jit(solution)/shard_map/rh,rhde->hde/dot_general | solution.py:122
  271.8 2.7 fusion.20
  274.9 1.7 fusion.15
  277.9 1.6 fusion.16
  (77 shorter events, 16.0 us)
Async XLA Ops:
  7.2 77.1 %copy-start.11 = (bf16[512,512]{1,0:T(8,128)(2,1)S(1)}, bf16[512,512]{1,0:T(8,128)(2,1)}, u32[]{:S(2)}) copy-start(bf16[512,512]{1,0:T(8,128)(2,1)} %param.5) | copy-start | bytes 1572868
  7.2 77.6 %copy-start.10 = (bf16[512,512]{1,0:T(8,128)(2,1)S(1)}, bf16[512,512]{1,0:T(8,128)(2,1)}, u32[]{:S(2)}) copy-start(bf16[512,512]{1,0:T(8,128)(2,1)} %param.8) | copy-start | bytes 1572868
  7.2 110.3 %all-gather.8.cloned.1.call-start = ((), (), s32[]{:S(2)}) async-start(), calls=%async_computation | async-start | bytes 8650752 | tf_op jit(solution)/shard_map/all_gather | solution.py:59
  12.1 1.1 copy-start.4
  16.3 243.5 %all-gather.10.cloned.1.call-start = ((), (), s32[]{:S(2)}) async-start(), calls=%async_computation.1 | async-start | bytes 8650752 | tf_op jit(solution)/shard_map/all_gather | solution.py:115
  84.7 45.0 %copy-start.2 = (bf16[4,128,4,128]{1,3,2,0:T(8,128)(2,1)}, bf16[4,128,4,128]{1,3,2,0:T(8,128)(2,1)S(1)}, u32[]{:S(2)}) copy-start(bf16[4,128,4,128]{1,3,2,0:T(8,128)(2,1)S(1)} %copy.116) | copy-start | bytes 1572868
  88.4 0.8 copy-start.8
  117.5 12.2 %copy-start.5 = (f32[4,4,128,128]{3,2,1,0:T(8,128)S(1)}, f32[4,4,128,128]{3,2,1,0:T(8,128)}, u32[]{:S(2)}) copy-start(f32[4,4,128,128]{3,2,1,0:T(8,128)} %copy-done.4) | copy-start | bytes 3145732
  117.5 14.9 %copy-start.6 = (f32[4,128,4,128]{1,3,2,0:T(8,128)S(1)}, f32[4,128,4,128]{1,3,2,0:T(8,128)}, u32[]{:S(2)}) copy-start(f32[4,128,4,128]{1,3,2,0:T(8,128)} %convolution_bitcast_fusion.9) | copy-start | bytes 3145732
  132.4 1.7 copy-start.7
  161.1 0.8 copy-start
  161.9 16.9 %copy-start.3 = (bf16[4,128,4,128]{1,3,2,0:T(8,128)(2,1)S(1)}, bf16[4,128,4,128]{1,3,2,0:T(8,128)(2,1)}, u32[]{:S(2)}) copy-start(bf16[4,128,4,128]{1,3,2,0:T(8,128)(2,1)} %copy-done.2) | copy-start | bytes 1572868
  163.5 12.7 %copy-start.1 = (bf16[4,128,4,128]{1,3,2,0:T(8,128)(2,1)S(1)}, bf16[4,128,4,128]{1,3,2,0:T(8,128)(2,1)}, u32[]{:S(2)}) copy-start(bf16[4,128,4,128]{1,3,2,0:T(8,128)(2,1)} %copy-done) | copy-start | bytes 1572868
  168.4 0.8 copy-start.9
Sparse Core Ops, SparseCore 0:
  16.4 101.0 all-gather.7
  166.7 92.9 all-gather.9
